TPU v7x, 256 devices: a whole 4x4x8 slice. The times are simulated.
256 devices in a mesh: dp: 64 (over y, z, core), tensor: 4 (over x).
Axes of the slice: x: 4, y: 4, z: 8, core: 2. Of those that a mesh axis runs over, the one named last changes fastest.
Arguments:
- query: bfloat16 [4096, 2560], P('dp', 'tensor'), may hold values from -18 to 18
- new_kv: bfloat16 [2, 4096, 512], P(None, 'dp', 'tensor'), may hold values from -7 to 7
- key_value_pages: bfloat16 [2, 6080, 128, 512], P(None, 'dp', None, 'tensor'), may hold values from -7 to 7
- page_table: int32 [4096, 32], P('dp'), may hold values from 0 to 6079, as said below
- cache_len: int32 [4096], P('dp'), may hold values from 1 to 4096, as said below
- residual: bfloat16 [4096, 2560], P('dp'), may hold values from -6 to 6
- out_weight: bfloat16 [2560, 2560], P('tensor'), may hold values from -0.125 to 0.125
- norm_gain: float32 [2560], replicated, may hold values from 0.25 to 1.75
- expert_ids: int32 [4096, 6], P('dp'), may hold values from 0 to 63, all different within a row; in each aligned block of 64 rows (0 to 63, 64 to 127, ...) at most 9 rows name the same one
- combine_weights: float32 [4096, 6], P('dp'), may hold values from 0.1 to 1
- expert_w1: bfloat16 [64, 2560, 2, 1536], P('dp', None, None, 'tensor'), may hold values from -0.125 to 0.125
- expert_w2: bfloat16 [64, 1536, 2560], P('dp', 'tensor'), may hold values from -0.15625 to 0.15625
Outputs:
- layer_out: bfloat16 [4096, 2560], P('dp', 'tensor')
Inputs may be any that keep to these rules, and one draw needn't show every extreme that they name: `page_table`: entry j of a request's row is the page holding its cache positions j * 128 to (j + 1) * 128 - 1; the pages of request r are among the 95 pages from (r // 64) * 95 on; no page serves two requests; entries past the last used page repeat it. `cache_len`: 6 requests, in 6 different blocks of 64 requests, hold more than (31) * 128 tokens, one of them exactly 4096; all others hold fewer than 64. `expert_ids`: each row names 6 different experts; among the rows of one device (aligned blocks of 64 rows) no expert is named more than 9 times.
All inputs are finite; a program needn't handle non-finite values.
Results may differ from a plain program's by a relative error of at most 0.012.
Values may be sent and summed in bfloat16 or wider, within the bound.
No kernel may reach another device: no remote copies, remote signals or barrier semaphores. Data moves between devices by JAX's collectives and lax.ppermute only.
A program may use at most 128 MiB of HBM per device.

v0:
```python
import math
import jax
import jax.numpy as jnp
from jax import lax
from jax.sharding import PartitionSpec as P

HEAD_SIZE = 128


def local_attention(query, new_kv, key_value_pages, page_table, cache_len):
    row_count = query.shape[0]
    pool_pages = key_value_pages.shape[1]
    page_size = key_value_pages.shape[2]
    head_dim = HEAD_SIZE
    local_heads = new_kv.shape[2] // head_dim
    group_heads = query.shape[1] // (local_heads * head_dim)
    table_width = page_table.shape[1]
    scale_of_score = 1.0 / math.sqrt(head_dim)
    local_pages = page_table - lax.axis_index("dp") * pool_pages
    used_pages = (cache_len + page_size - 1) // page_size
    slot_ids = jnp.arange(table_width, dtype=jnp.int32)
    live_slot = slot_ids[None, :] < used_pages[:, None]
    page_ids = jnp.arange(pool_pages, dtype=jnp.int32)
    onehot = ((local_pages[:, :, None] == page_ids[None, None, :]) & live_slot[:, :, None]).astype(
        jnp.float32
    )
    owner = jnp.sum(onehot, axis=1)
    page_slot = jnp.sum(onehot * slot_ids.astype(jnp.float32)[None, :, None], axis=(0, 1))
    page_len = jnp.dot(cache_len.astype(jnp.float32), owner, precision=lax.Precision.HIGHEST)
    q_pages = jnp.dot(owner.T.astype(jnp.bfloat16), query, preferred_element_type=jnp.float32)
    q_pages = q_pages.astype(jnp.bfloat16).reshape(pool_pages, local_heads, group_heads, head_dim)
    keys_of_page = key_value_pages[0].reshape(pool_pages, page_size, local_heads, head_dim)
    values_of_page = key_value_pages[1].reshape(pool_pages, page_size, local_heads, head_dim)
    scores = (
        jnp.einsum("pkgd,pikd->pkgi", q_pages, keys_of_page, preferred_element_type=jnp.float32)
        * scale_of_score
    )
    position = page_slot[:, None] * page_size + jnp.arange(page_size, dtype=jnp.float32)[None, :]
    valid = position < page_len[:, None]
    scores = jnp.where(valid[:, None, None, :], scores, -1e30)
    page_max = jnp.max(scores, axis=3)
    own_heads = query.reshape(row_count, local_heads, group_heads, head_dim)
    new_keys = new_kv[0].reshape(row_count, local_heads, head_dim)
    new_values = new_kv[1].reshape(row_count, local_heads, head_dim)
    fresh_score = (
        jnp.einsum("rkgd,rkd->rkg", own_heads, new_keys, preferred_element_type=jnp.float32)
        * scale_of_score
    )
    request_max = jnp.max(jnp.where(owner[:, :, None, None] > 0, page_max[None], -1e30), axis=1)
    row_max = jnp.maximum(request_max, fresh_score)
    page_top = jnp.dot(owner.T, row_max.reshape(row_count, -1), precision=lax.Precision.HIGHEST)
    page_top = page_top.reshape(pool_pages, local_heads, group_heads)
    weights = jnp.where(valid[:, None, None, :], jnp.exp(scores - page_top[..., None]), 0.0)
    page_den = jnp.sum(weights, axis=3).reshape(pool_pages, -1)
    page_num = jnp.einsum(
        "pkgi,pikd->pkgd",
        weights.astype(jnp.bfloat16),
        values_of_page,
        preferred_element_type=jnp.float32,
    ).reshape(pool_pages, -1)
    weight_new = jnp.exp(fresh_score - row_max)
    denominator = jnp.dot(owner, page_den, precision=lax.Precision.HIGHEST).reshape(
        row_count, local_heads, group_heads
    )
    denominator = denominator + weight_new
    weighted_numerator = jnp.dot(owner, page_num, precision=lax.Precision.HIGHEST)
    weighted_numerator = weighted_numerator.reshape(row_count, local_heads, group_heads, head_dim)
    weighted_numerator = weighted_numerator + jnp.einsum(
        "rkg,rkd->rkgd",
        weight_new.astype(jnp.bfloat16),
        new_values,
        preferred_element_type=jnp.float32,
    )
    return (weighted_numerator / denominator[..., None]).reshape(row_count, -1).astype(jnp.bfloat16)


def per_device(
    query,
    new_kv,
    key_value_pages,
    page_table,
    cache_len,
    residual,
    out_weight,
    norm_gain,
    expert_ids,
    combine_weights,
    expert_w1,
    expert_w2,
):
    attn = local_attention(query, new_kv, key_value_pages, page_table, cache_len)
    partial_proj = jnp.dot(attn, out_weight, preferred_element_type=jnp.float32)
    row_count, model_width = residual.shape
    share_width = model_width // lax.axis_size("tensor")
    share_start = lax.axis_index("tensor") * share_width
    summed = lax.psum(partial_proj, "tensor")
    state = residual.astype(jnp.float32) + summed
    mean_square = jnp.mean(state * state, axis=1, keepdims=True)
    normed = (state * lax.rsqrt(mean_square + 1e-05) * norm_gain).astype(jnp.bfloat16)
    state_share = lax.dynamic_slice_in_dim(state, share_start, share_width, 1)
    local_experts = expert_w1.shape[0]
    top_count = expert_ids.shape[1]
    experts = local_experts * lax.axis_size("dp")
    capacity = min(
        row_count, max(3, (3 * row_count * top_count + 2 * experts - 1) // (2 * experts))
    )
    flat_ids = expert_ids.reshape(-1)
    choice_rows = flat_ids.shape[0]
    row_iota = jnp.arange(choice_rows, dtype=jnp.int32)
    choice_hot = (flat_ids[:, None] == jnp.arange(experts, dtype=jnp.int32)[None, :]).astype(
        jnp.float32
    )
    strictly_lower = (row_iota[:, None] > row_iota[None, :]).astype(jnp.float32)
    earlier = jnp.dot(strictly_lower, choice_hot, precision=lax.Precision.HIGHEST)
    slot_rank = jnp.sum(earlier * choice_hot, axis=1).astype(jnp.int32)
    slot_index = flat_ids * capacity + slot_rank
    slot_hot = (
        slot_index[:, None] == jnp.arange(experts * capacity, dtype=jnp.int32)[None, :]
    ).astype(jnp.float32)
    token_hot = (
        (row_iota // top_count)[:, None] == jnp.arange(row_count, dtype=jnp.int32)[None, :]
    ).astype(jnp.float32)
    placing = jnp.dot(slot_hot.T, token_hot, precision=lax.Precision.HIGHEST)
    outgoing = jnp.dot(placing.astype(jnp.bfloat16), normed, preferred_element_type=jnp.float32)
    outgoing = outgoing.astype(jnp.bfloat16).reshape(experts, capacity, -1)
    mixing = jnp.dot(
        token_hot.T,
        slot_hot * combine_weights.reshape(-1)[:, None],
        precision=lax.Precision.HIGHEST,
    )
    arrived = lax.all_to_all(outgoing, "dp", split_axis=0, concat_axis=0, tiled=True)
    sources = arrived.shape[0] // local_experts
    item_count = arrived.shape[1]
    arrived_rows = arrived.reshape(sources, local_experts, item_count, model_width)
    gate_up = jnp.einsum(
        "send,edcf->sencf", arrived_rows, expert_w1, preferred_element_type=jnp.float32
    )
    activated = (jax.nn.silu(gate_up[..., 0, :]) * gate_up[..., 1, :]).astype(jnp.bfloat16)
    partial_out = jnp.einsum(
        "senf,efd->send", activated, expert_w2, preferred_element_type=jnp.float32
    )
    partial_out = partial_out.reshape(sources * local_experts, item_count, model_width)
    expert_sum = lax.psum_scatter(
        partial_out.astype(jnp.bfloat16), "tensor", scatter_dimension=2, tiled=True
    )
    returned_rows = lax.all_to_all(expert_sum, "dp", split_axis=0, concat_axis=0, tiled=True)
    expert_mix = jnp.dot(
        mixing,
        returned_rows.reshape(experts * capacity, -1).astype(jnp.float32),
        precision=lax.Precision.HIGHEST,
    )
    return (state_share + expert_mix).astype(jnp.bfloat16)


def solution(mesh):
    return jax.shard_map(
        per_device,
        mesh=mesh,
        in_specs=(
            P("dp", "tensor"),
            P(None, "dp", "tensor"),
            P(None, "dp", None, "tensor"),
            P("dp", None),
            P("dp"),
            P("dp", None),
            P("tensor", None),
            P(),
            P("dp", None),
            P("dp", None),
            P("dp", None, None, "tensor"),
            P("dp", "tensor", None),
        ),
        out_specs=P("dp", "tensor"),
        check_vma=False,
    )
```

profile of v0, /device:TPU:1, one launch (start us, length us, event | category | flops | bytes accessed | tf_op | source)
XLA Modules:
  0.0 362.5 jit_solution(4747731906453002867)
XLA Ops:
  10.4 1.7 convolution_convert_fusion.2
  12.2 1.6 reshape.226
  15.0 4.4 %fusion.69 = (f32[95,5]{1,0:T(8,128)S(1)}, f32[95,5,128]{2,1,0:T(8,128)}) fusion(bf16[95,5,128]{2,1,0:T(8,128)(2,1)S(1)} %reshape.224, bf16[2,95,128,128]{3,2,1,0:T(8,128)(2,1)} %param.14, pred[95,128]{1,0:T(8,128)(4,1)S(1)} %add_compare_fusion), kind=kOutput, calls=%fused_computation.101 | convolution fusion | flops 15746725 | bytes 3491820 | tf_op jit(solution)/shard_map/pkgd,pikd->pkgi/dot_general | solution.py:35
  19.4 1.4 bitcast_convert_fusion
  23.1 1.3 fusion.39
  24.4 3.0 fusion.3
  29.7 1.4 fusion.25
  31.1 1.6 fusion.48
  33.6 49.5 %all-reduce.2.cloned.1.call-done = f32[64,2560]{1,0:T(8,128)} async-done(((f32[64,2560]{1,0:T(8,128)}), f32[64,2560]{1,0:T(8,128)}) %all-reduce.2.cloned.1.call-update) | async-done | bytes 655376 | tf_op jit(solution)/shard_map/psum | solution.py:96
  83.1 1.4 multiply_reduce_fusion
  85.3 2.5 convolution_convert_fusion.1
  87.9 5.1 %reshape.232 = bf16[64,9,2560]{2,1,0:T(8,128)(2,1)} reshape(bf16[576,2560]{1,0:T(8,128)(2,1)} %convolution_convert_fusion.1) | data formatting | bytes 5898240 | tf_op jit(solution)/shard_map/reshape | solution.py:125
  93.0 131.8 %all_to_all.10 = bf16[64,9,2560]{2,1,0:T(8,128)(2,1)S(1)} all-to-all(bf16[64,9,2560]{2,1,0:T(8,128)(2,1)} %reshape.232), channel_id=1, replica_groups=mesh['dp'=64,'tensor'=4] {'dp'}, dimensions={0} | all-to-all | bytes 5898240 | tf_op jit(solution)/shard_map/all_to_all | solution.py:131
  224.8 5.0 %fusion.11 = f32[64,1,9,2,384]{4,0,3,2,1:T(8,128)S(1)} fusion(bf16[2560,2,384]{2,1,0:T(2,128)(2,1)S(1)} %bitcast.90, bf16[64,9,2560,1]{2,1,0,3:T(8,128)(2,1)S(1)} %bitcast.87), kind=kOutput, calls=%fused_computation.13 | convolution fusion | flops 2264924160 | bytes 8650752 | tf_op jit(solution)/shard_map/send,edcf->sencf/dot_general | solution.py:135
  229.8 3.4 convolution_convert_fusion
  233.2 12.2 %copy.60 = bf16[64,9,2560]{0,1,2:T(8,128)(2,1)} copy(bf16[64,9,2560]{2,0,1:T(8,128)(2,1)} %convolution_convert_fusion) | data formatting | bytes 5898240
  245.3 12.7 %reshape.245 = bf16[2560,576]{1,0:T(8,128)(2,1)} reshape(bf16[2560,9,64]{2,1,0:T(8,128)(2,1)} %bitcast.85) | data formatting | bytes 5898240
  258.1 37.9 %reduce-scatter.4.cloned.1.call-done = bf16[640,576]{1,0:T(8,128)(2,1)} async-done(((bf16[2560,576]{1,0:T(8,128)(2,1)}), bf16[640,576]{1,0:T(8,128)(2,1)}) %reduce-scatter.4.cloned.1.call-update) | async-done | bytes 737296
  295.9 3.9 %reshape.246 = bf16[640,9,64]{2,1,0:T(8,128)(2,1)} reshape(bf16[640,576]{1,0:T(8,128)(2,1)} %reduce-scatter.4.cloned.1.call-done) | data formatting | bytes 1474560
  299.9 6.2 %copy.53 = bf16[64,9,640]{2,1,0:T(8,128)(2,1)} copy(bf16[64,9,640]{0,1,2:T(8,128)(2,1)} %bitcast.86) | data formatting | bytes 1474560 | tf_op jit(solution)/shard_map/reduce_scatter | solution.py:143
  306.1 10.9 %all-to-all-start.1 = ((bf16[64,9,640]{2,1,0:T(8,128)(2,1)}), bf16[64,9,640]{2,1,0:T(8,128)(2,1)}, u32[]{:S(2)}, u32[]{:S(2)}) async-start(bf16[64,9,640]{2,1,0:T(8,128)(2,1)} %copy.53), calls=%async_computation.1 | async-start | bytes 2621440 | tf_op jit(solution)/shard_map/all_to_all | solution.py:146
  318.0 33.1 %all-to-all-done.1 = bf16[64,9,640]{2,1,0:T(8,128)(2,1)} async-done(((bf16[64,9,640]{2,1,0:T(8,128)(2,1)}), bf16[64,9,640]{2,1,0:T(8,128)(2,1)}, u32[]{:S(2)}, u32[]{:S(2)}) %all-to-all-start.1) | async-done | bytes 737312 | tf_op jit(solution)/shard_map/all_to_all | solution.py:146
  351.1 2.3 reshape.235
  353.4 2.3 fusion.24
  (50 shorter events, 12.4 us)
Async XLA Ops:
  6.5 24.5 %copy-start = (bf16[640,2560]{1,0:T(8,128)(2,1)S(1)}, bf16[640,2560]{1,0:T(8,128)(2,1)}, u32[]{:S(2)}) copy-start(bf16[640,2560]{1,0:T(8,128)(2,1)} %param.18) | copy-start | bytes 9830404
  6.5 76.6 %all-reduce.2.cloned.1.call-start = ((), (), s32[]{:S(2)}) async-start(), calls=%async_computation.3 | async-start | bytes 1310720 | tf_op jit(solution)/shard_map/psum | solution.py:96
  15.0 4.4 %copy-start.2 = (pred[95,128]{1,0:T(8,128)(4,1)}, pred[95,128]{1,0:T(8,128)(4,1)S(1)}, u32[]{:S(2)}) copy-start(pred[95,128]{1,0:T(8,128)(4,1)S(1)} %add_compare_fusion) | copy-start | bytes 36484
  29.7 3.0 copy-start.4
  31.0 54.3 %copy-start.3 = (f32[2560]{0:T(1024)S(1)}, f32[2560]{0:T(1024)}, u32[]{:S(2)}) copy-start(f32[2560]{0:T(1024)} %param.19) | copy-start | bytes 30724
  32.6 263.3 %reduce-scatter.4.cloned.1.call-start = ((), (), s32[]{:S(2)}) async-start(), calls=%async_computation.4 | async-start | bytes 4096000
  84.5 0.9 copy-start.1
  93.0 131.8 %copy-start.6 = (bf16[1,2560,2,384]{3,2,1,0:T(2,128)(2,1)S(1)}, bf16[1,2560,2,384]{3,2,1,0:T(2,128)(2,1)}, u32[]{:S(2)}) copy-start(bf16[1,2560,2,384]{3,2,1,0:T(2,128)(2,1)} %param.22) | copy-start | bytes 11796484
  224.8 5.0 %copy-start.7 = (bf16[1,384,2560]{2,1,0:T(8,128)(2,1)S(1)}, bf16[1,384,2560]{2,1,0:T(8,128)(2,1)}, u32[]{:S(2)}) copy-start(bf16[1,384,2560]{2,1,0:T(8,128)(2,1)} %param.23) | copy-start | bytes 5898244
  299.9 17.2 %copy-start.5 = (f32[64,6]{0,1:T(8,128)S(1)}, f32[64,6]{0,1:T(8,128)}, u32[]{:S(2)}) copy-start(f32[64,6]{0,1:T(8,128)} %param.21) | copy-start | bytes 4612
  306.1 45.0 %all-to-all-start.1 = ((bf16[64,9,640]{2,1,0:T(8,128)(2,1)}), bf16[64,9,640]{2,1,0:T(8,128)(2,1)}, u32[]{:S(2)}, u32[]{:S(2)}) async-start(bf16[64,9,640]{2,1,0:T(8,128)(2,1)} %copy.53), calls=%async_computation.1 | async-start | bytes 2621440 | tf_op jit(solution)/shard_map/all_to_all | solution.py:146
Sparse Core Ops, SparseCore 0:
  32.8 50.2 all-reduce.1
  258.2 37.6 reduce-scatter.3
where the time goes:
time: 364 us; the launch traced here: 362 us
  blocking collectives  132 us (36%)
  waiting for transfers between devices  121 us (33%)
  local copies, waits for them, and re-layouts  47.5 us (13%)
  matrix products  29.5 us (8%)
  between operations  13.6 us (4%)
  starting transfers between devices  11 us (3%)
  other arithmetic  8.57 us (2%)
    all_to_all x1, blocking collectives, per_device(): lax.all_to_all(outgoing, 'dp', split_axis=0, concat_axis=0, tiled=True)  132 us
    psum x1, waiting for transfers between devices, per_device(): summed = lax.psum(partial_proj, 'tensor')  49.5 us
    unnamed x3, waiting for transfers between devices  37.9 us
    all_to_all x1, waiting for transfers between devices, per_device(): lax.all_to_all(expert_sum, 'dp', split_axis=0, concat_axis=0, tiled=True)  33.1 us
    unnamed x23, local copies, waits for them, and re-layouts  29.9 us
    all_to_all x1, starting transfers between devices, per_device(): lax.all_to_all(expert_sum, 'dp', split_axis=0, concat_axis=0, tiled=True)  10.9 us
  transfers between devices with their start and end apart: 3, of which 3 were waited for; matrix products, arithmetic and copies ran while one was open for 1% of the time, Pallas kernels for 0%

commit v1 on v0

--- a/solution.py
+++ b/solution.py
@@ -93,7 +93,9 @@
     row_count, model_width = residual.shape
     share_width = model_width // lax.axis_size("tensor")
     share_start = lax.axis_index("tensor") * share_width
-    summed = lax.psum(partial_proj, "tensor")
+    summed = partial_proj
+    for hop in (1, 2):
+        summed = summed + lax.ppermute(summed, "tensor", [(dev, dev ^ hop) for dev in range(4)])
     state = residual.astype(jnp.float32) + summed
     mean_square = jnp.mean(state * state, axis=1, keepdims=True)
     normed = (state * lax.rsqrt(mean_square + 1e-05) * norm_gain).astype(jnp.bfloat16)

time: 364 us -> 349 us (0.959)
  waiting for transfers between devices: 121 us -> 97.9 us
  starting transfers between devices: 11 us -> 17 us
    psum x1 -> x0, waiting for transfers between devices: 49.5 us -> none  [per_device(): summed = lax.psum(partial_proj, 'tensor')]
    ppermute x0 -> x2, waiting for transfers between devices: none -> 25.9 us  [per_device(): lax.ppermute(summed, 'tensor', [(dev, dev ^ hop) for dev in range(4)])]
    ppermute x0 -> x2, starting transfers between devices: none -> 6.07 us  [per_device(): lax.ppermute(summed, 'tensor', [(dev, dev ^ hop) for dev in range(4)])]
    unnamed x3 -> x2, waiting for transfers between devices: 37.9 us -> 38.8 us
  transfers between devices with their start and end apart: 3 -> 4, of which waited for: 3 -> 4; matrix products, arithmetic and copies ran while one was open for 1% -> 1% of each run, Pallas kernels for 0% -> 0%
where the time goes in v1:
time: 349 us; the launch traced here: 347 us
  blocking collectives  133 us (38%)
  waiting for transfers between devices  97.9 us (28%)
  local copies, waits for them, and re-layouts  47.5 us (14%)
  matrix products  28.7 us (8%)
  starting transfers between devices  17 us (5%)
  between operations  13.6 us (4%)
  other arithmetic  9.69 us (3%)
    all_to_all x1, blocking collectives, per_device(): lax.all_to_all(outgoing, 'dp', split_axis=0, concat_axis=0, tiled=True)  133 us
    unnamed x2, waiting for transfers between devices  38.8 us
    all_to_all x1, waiting for transfers between devices, per_device(): lax.all_to_all(expert_sum, 'dp', split_axis=0, concat_axis=0, tiled=True)  33.1 us
    unnamed x23, local copies, waits for them, and re-layouts  29.9 us
    ppermute x2, waiting for transfers between devices, per_device(): lax.ppermute(summed, 'tensor', [(dev, dev ^ hop) for dev in range(4)])  25.9 us
    all_to_all x1, starting transfers between devices, per_device(): lax.all_to_all(expert_sum, 'dp', split_axis=0, concat_axis=0, tiled=True)  10.9 us
  transfers between devices with their start and end apart: 4, of which 4 were waited for; matrix products, arithmetic and copies ran while one was open for 1% of the time, Pallas kernels for 0%

profile of v1, /device:TPU:1, one launch (start us, length us, event | category | flops | bytes accessed | tf_op | source)
XLA Modules:
  0.0 347.2 jit_solution(9210924670732735576)
XLA Ops:
  10.4 1.7 convolution_convert_fusion.2
  12.2 1.6 reshape.226
  15.0 4.4 %fusion.68 = (f32[95,5]{1,0:T(8,128)S(1)}, f32[95,5,128]{2,1,0:T(8,128)}) fusion(bf16[95,5,128]{2,1,0:T(8,128)(2,1)S(1)} %reshape.224, bf16[2,95,128,128]{3,2,1,0:T(8,128)(2,1)} %param.14, pred[95,128]{1,0:T(8,128)(4,1)S(1)} %add_compare_fusion), kind=kOutput, calls=%fused_computation.100 | convolution fusion | flops 15746725 | bytes 3491820 | tf_op jit(solution)/shard_map/pkgd,pikd->pkgi/dot_general | solution.py:35
  19.4 1.4 bitcast_convert_fusion
  24.4 3.0 fusion.3
  31.8 2.1 collective-permute-start
  33.9 13.2 %collective-permute-done = f32[64,2560]{1,0:T(8,128)S(1)} collective-permute-done((f32[64,2560]{1,0:T(8,128)S(1)}, f32[64,2560]{1,0:T(8,128)S(1)}, u32[]{:S(2)}, u32[]{:S(2)}) %collective-permute-start) | collective-permute-done | bytes 655392 | tf_op jit(solution)/shard_map/ppermute | solution.py:98
  48.0 3.9 %collective-permute-start.1 = (f32[64,2560]{1,0:T(8,128)}, f32[64,2560]{1,0:T(8,128)}, u32[]{:S(2)}, u32[]{:S(2)}) collective-permute-start(f32[64,2560]{1,0:T(8,128)} %add.84), channel_id=1, source_target_pairs={{0,2},{1,3},{2,0},{3,1},{4,6},{5,7},{6,4},{7,5},{8,10},{9,11},{10,... | collective-permute-start | bytes 1966088 | tf_op jit(solution)/shard_map/ppermute | solution.py:98
  52.8 12.7 %collective-permute-done.1 = f32[64,2560]{1,0:T(8,128)} collective-permute-done((f32[64,2560]{1,0:T(8,128)}, f32[64,2560]{1,0:T(8,128)}, u32[]{:S(2)}, u32[]{:S(2)}) %collective-permute-start.1) | collective-permute-done | bytes 655392 | tf_op jit(solution)/shard_map/ppermute | solution.py:98
  65.5 1.6 multiply_reduce_fusion
  68.0 2.5 convolution_convert_fusion.1
  70.5 5.1 %reshape.232 = bf16[64,9,2560]{2,1,0:T(8,128)(2,1)} reshape(bf16[576,2560]{1,0:T(8,128)(2,1)} %convolution_convert_fusion.1) | data formatting | bytes 5898240 | tf_op jit(solution)/shard_map/reshape | solution.py:127
  75.6 132.9 %all_to_all.10 = bf16[64,9,2560]{2,1,0:T(8,128)(2,1)S(1)} all-to-all(bf16[64,9,2560]{2,1,0:T(8,128)(2,1)} %reshape.232), channel_id=1, replica_groups=mesh['dp'=64,'tensor'=4] {'dp'}, dimensions={0} | all-to-all | bytes 5898240 | tf_op jit(solution)/shard_map/all_to_all | solution.py:133
  208.6 5.0 %fusion.11 = f32[64,1,9,2,384]{4,0,3,2,1:T(8,128)S(1)} fusion(bf16[2560,2,384]{2,1,0:T(2,128)(2,1)S(1)} %bitcast.90, bf16[64,9,2560,1]{2,1,0,3:T(8,128)(2,1)S(1)} %bitcast.87), kind=kOutput, calls=%fused_computation.13 | convolution fusion | flops 2264924160 | bytes 8650752 | tf_op jit(solution)/shard_map/send,edcf->sencf/dot_general | solution.py:137
  213.6 3.4 convolution_convert_fusion
  217.0 12.2 %copy.60 = bf16[64,9,2560]{0,1,2:T(8,128)(2,1)} copy(bf16[64,9,2560]{2,0,1:T(8,128)(2,1)} %convolution_convert_fusion) | data formatting | bytes 5898240
  229.2 12.7 %reshape.245 = bf16[2560,576]{1,0:T(8,128)(2,1)} reshape(bf16[2560,9,64]{2,1,0:T(8,128)(2,1)} %bitcast.85) | data formatting | bytes 5898240
  241.9 38.8 %reduce-scatter.4.cloned.1.call-done = bf16[640,576]{1,0:T(8,128)(2,1)} async-done(((bf16[2560,576]{1,0:T(8,128)(2,1)}), bf16[640,576]{1,0:T(8,128)(2,1)}) %reduce-scatter.4.cloned.1.call-update) | async-done | bytes 737296
  280.7 3.9 %reshape.246 = bf16[640,9,64]{2,1,0:T(8,128)(2,1)} reshape(bf16[640,576]{1,0:T(8,128)(2,1)} %reduce-scatter.4.cloned.1.call-done) | data formatting | bytes 1474560
  284.6 6.2 %copy.53 = bf16[64,9,640]{2,1,0:T(8,128)(2,1)} copy(bf16[64,9,640]{0,1,2:T(8,128)(2,1)} %bitcast.86) | data formatting | bytes 1474560 | tf_op jit(solution)/shard_map/reduce_scatter | solution.py:145
  290.9 10.9 %all-to-all-start.1 = ((bf16[64,9,640]{2,1,0:T(8,128)(2,1)}), bf16[64,9,640]{2,1,0:T(8,128)(2,1)}, u32[]{:S(2)}, u32[]{:S(2)}) async-start(bf16[64,9,640]{2,1,0:T(8,128)(2,1)} %copy.53), calls=%async_computation.1 | async-start | bytes 2621440 | tf_op jit(solution)/shard_map/all_to_all | solution.py:148
  302.7 33.1 %all-to-all-done.1 = bf16[64,9,640]{2,1,0:T(8,128)(2,1)} async-done(((bf16[64,9,640]{2,1,0:T(8,128)(2,1)}), bf16[64,9,640]{2,1,0:T(8,128)(2,1)}, u32[]{:S(2)}, u32[]{:S(2)}) %all-to-all-start.1) | async-done | bytes 737312 | tf_op jit(solution)/shard_map/all_to_all | solution.py:148
  335.9 2.3 reshape.235
  338.1 2.3 add_convert_fusion
  (52 shorter events, 16.6 us)
Async XLA Ops:
  6.5 24.5 %copy-start = (bf16[640,2560]{1,0:T(8,128)(2,1)S(1)}, bf16[640,2560]{1,0:T(8,128)(2,1)}, u32[]{:S(2)}) copy-start(bf16[640,2560]{1,0:T(8,128)(2,1)} %param.18) | copy-start | bytes 9830404
  6.5 274.2 %reduce-scatter.4.cloned.1.call-start = ((), (), s32[]{:S(2)}) async-start(), calls=%async_computation.3 | async-start | bytes 4096000
  15.0 4.4 %copy-start.2 = (pred[95,128]{1,0:T(8,128)(4,1)}, pred[95,128]{1,0:T(8,128)(4,1)S(1)}, u32[]{:S(2)}) copy-start(pred[95,128]{1,0:T(8,128)(4,1)S(1)} %add_compare_fusion) | copy-start | bytes 36484
  29.7 22.2 %copy-start.4 = (s32[64,6]{0,1:T(8,128)S(1)}, s32[64,6]{0,1:T(8,128)}, u32[]{:S(2)}) copy-start(s32[64,6]{0,1:T(8,128)} %param.20) | copy-start | bytes 4612
  31.7 36.2 %copy-start.3 = (f32[2560]{0:T(1024)S(1)}, f32[2560]{0:T(1024)}, u32[]{:S(2)}) copy-start(f32[2560]{0:T(1024)} %param.19) | copy-start | bytes 30724
  31.8 15.3 %collective-permute-start = (f32[64,2560]{1,0:T(8,128)S(1)}, f32[64,2560]{1,0:T(8,128)S(1)}, u32[]{:S(2)}, u32[]{:S(2)}) collective-permute-start(f32[64,2560]{1,0:T(8,128)S(1)} %fusion.47), channel_id=1, source_target_pairs={{0,1},{1,0},{2,3},{3,2},{4,5},{5,4},{6,7},{7,6},{8,9},{9,8},{10,11... | collective-permute-start | bytes 1966088 | tf_op jit(solution)/shard_map/ppermute | solution.py:98
  48.0 17.6 %collective-permute-start.1 = (f32[64,2560]{1,0:T(8,128)}, f32[64,2560]{1,0:T(8,128)}, u32[]{:S(2)}, u32[]{:S(2)}) collective-permute-start(f32[64,2560]{1,0:T(8,128)} %add.84), channel_id=1, source_target_pairs={{0,2},{1,3},{2,0},{3,1},{4,6},{5,7},{6,4},{7,5},{8,10},{9,11},{10,... | collective-permute-start | bytes 1966088 | tf_op jit(solution)/shard_map/ppermute | solution.py:98
  67.1 0.9 copy-start.1
  75.6 132.9 %copy-start.6 = (bf16[1,2560,2,384]{3,2,1,0:T(2,128)(2,1)S(1)}, bf16[1,2560,2,384]{3,2,1,0:T(2,128)(2,1)}, u32[]{:S(2)}) copy-start(bf16[1,2560,2,384]{3,2,1,0:T(2,128)(2,1)} %param.22) | copy-start | bytes 11796484
  208.6 5.0 %copy-start.7 = (bf16[1,384,2560]{2,1,0:T(8,128)(2,1)S(1)}, bf16[1,384,2560]{2,1,0:T(8,128)(2,1)}, u32[]{:S(2)}) copy-start(bf16[1,384,2560]{2,1,0:T(8,128)(2,1)} %param.23) | copy-start | bytes 5898244
  284.6 17.2 %copy-start.5 = (f32[64,6]{0,1:T(8,128)S(1)}, f32[64,6]{0,1:T(8,128)}, u32[]{:S(2)}) copy-start(f32[64,6]{0,1:T(8,128)} %param.21) | copy-start | bytes 4612
  290.9 45.0 %all-to-all-start.1 = ((bf16[64,9,640]{2,1,0:T(8,128)(2,1)}), bf16[64,9,640]{2,1,0:T(8,128)(2,1)}, u32[]{:S(2)}, u32[]{:S(2)}) async-start(bf16[64,9,640]{2,1,0:T(8,128)(2,1)} %copy.53), calls=%async_computation.1 | async-start | bytes 2621440 | tf_op jit(solution)/shard_map/all_to_all | solution.py:148
Sparse Core Ops, SparseCore 0:
  242.0 38.6 reduce-scatter.3
